TPU v7x, 32 devices: a whole 2x2x4 slice. The times are simulated.
32 devices in a mesh: groups: 2 (over y), ctx: 4 (over z), head: 4 (over x, core).
Axes of the slice: x: 2, y: 2, z: 4, core: 2. Of those that a mesh axis runs over, the one named last changes fastest.
Arguments:
- queries: bfloat16 [8192, 512], P(('groups', 'ctx', 'head')), parts along dimension 0, may hold values from -8 to 8, as said below
- keys: bfloat16 [8192, 512], P(('groups', 'ctx', 'head')), parts along dimension 0, may hold values from -8 to 8
- values: bfloat16 [8192, 4096], P(('groups', 'ctx', 'head')), parts along dimension 0, may hold values from -6 to 6
- gain: float32 [4096], P('head'), may hold values from 0.5 to 1.5
Outputs:
- mixed: bfloat16 [8192, 4096], P(('groups', 'ctx', 'head')), parts along dimension 0
There are 2 independent parts, one for each index of `groups`. A program takes and returns all parts, laid end to end along the dimension named above; an argument that names none is the same for every part. Nothing has to cross between parts.
Inputs may be any that keep to these rules, and one draw needn't show every extreme that they name: `queries`: query entries lie in the stated range.
All inputs are finite; a program needn't handle non-finite values.
Results may differ from a plain program's by a relative error of at most 0.0054.
Values may be sent and summed in bfloat16 or wider, within the bound.
No kernel may reach another device: no remote copies, remote signals or barrier semaphores. Data moves between devices by JAX's collectives and lax.ppermute only.
A program may use at most 128 MiB of HBM per device.

v0:
```python
import math
import jax
import jax.numpy as jnp
from jax import lax
from jax.sharding import PartitionSpec as P

HEADS = 32
KD = 16
VD = 128
WINDOW = 64
outer_scale = 1.0 / (4.0 * math.sqrt(2.0))
epsilon = 1e-06


def shifted(shard, axis, by):
    peers = lax.axis_size(axis)
    pairs = [(i, i + by) for i in range(peers) if 0 <= i + by < peers]
    return lax.ppermute(shard, axis, pairs)


def entering(shard, axis, combine, identity):
    peers, here = (lax.axis_size(axis), lax.axis_index(axis))
    everything = lax.all_gather(shard, axis)
    start = jnp.broadcast_to(jnp.asarray(identity, shard.dtype), shard.shape)

    def hop(k, before):
        reached = k < here
        new = combine(before, everything[k])
        return jnp.where(reached, new, before)

    return lax.fori_loop(0, peers, hop, start)


def feature_map(vector):
    width = vector.shape[-1]
    products = (vector[..., :, None] * vector[..., None, :]).reshape(
        vector.shape[:-1] + (width * width,)
    )
    unit_column = jnp.ones(vector.shape[:-1] + (1,), jnp.float32)
    return jnp.concatenate([unit_column, vector * 0.5, products * outer_scale], axis=-1)


def per_device(queries, keys, values, gain):
    local_tokens = queries.shape[0]
    query_tok = queries.reshape(local_tokens, HEADS, KD)
    key_tok = keys.reshape(local_tokens, HEADS, KD)
    value_tok = values.reshape(local_tokens, HEADS, VD)
    query_head, key_head, value_head = (
        lax.all_to_all(query_tok, "head", split_axis=1, concat_axis=0, tiled=True),
        lax.all_to_all(key_tok, "head", split_axis=1, concat_axis=0, tiled=True),
        lax.all_to_all(value_tok, "head", split_axis=1, concat_axis=0, tiled=True),
    )
    span_rows = query_head.shape[0]
    heads_here = query_head.shape[1]
    block_rows = min(512, span_rows)
    block_count = span_rows // block_rows
    tail_keys, tail_values = shifted(
        (key_head[span_rows - WINDOW :], value_head[span_rows - WINDOW :]), "ctx", 1
    )
    key_ext = jnp.concatenate([tail_keys, key_head], axis=0)
    value_ext = jnp.concatenate([tail_values, value_head], axis=0)
    first_span = lax.axis_index("ctx") == 0
    key_features = feature_map(key_head.astype(jnp.float32)).astype(jnp.bfloat16)
    own_state = jnp.einsum(
        "bhf,bhv->hfv", key_features, value_head, preferred_element_type=jnp.float32
    )

    def combine_states(earlier, later):
        return earlier + later

    prefix = entering(own_state, "ctx", combine_states, jnp.zeros_like(own_state))

    def block_step(state, block_index):
        start = block_index * block_rows
        query_block = lax.dynamic_slice_in_dim(query_head, start, block_rows, 0)
        key_block = lax.dynamic_slice_in_dim(key_head, start, block_rows, 0)
        value_block = lax.dynamic_slice_in_dim(value_head, start, block_rows, 0)
        key_feat = lax.dynamic_slice_in_dim(key_features, start, block_rows, 0)
        key_window = lax.dynamic_slice_in_dim(key_ext, start, block_rows + WINDOW, 0)
        value_window = lax.dynamic_slice_in_dim(value_ext, start, block_rows + WINDOW, 0)
        scores = (
            jnp.einsum("bhd,chd->hbc", query_block, key_block, preferred_element_type=jnp.float32)
            * 0.25
        )
        row_pos = jnp.arange(block_rows)[:, None]
        col_pos = jnp.arange(block_rows)[None, :]
        kernel = jnp.where(col_pos <= row_pos, 1.0 + scores + 0.5 * scores * scores, 0.0).astype(
            jnp.bfloat16
        )
        intra = jnp.einsum("hbc,chv->bhv", kernel, value_block, preferred_element_type=jnp.float32)
        query_feat = feature_map(query_block.astype(jnp.float32)).astype(jnp.bfloat16)
        inter = jnp.einsum(
            "bhf,hfv->bhv",
            query_feat,
            state.astype(jnp.bfloat16),
            preferred_element_type=jnp.float32,
        )
        state = state + jnp.einsum(
            "bhf,bhv->hfv", key_feat, value_block, preferred_element_type=jnp.float32
        )
        window_scores = (
            jnp.einsum("bhd,chd->hbc", query_block, key_window, preferred_element_type=jnp.float32)
            * 0.25
        )
        key_pos = jnp.arange(block_rows + WINDOW)[None, :] - WINDOW
        valid = (
            (key_pos <= row_pos)
            & (key_pos > row_pos - WINDOW)
            & ((start + key_pos >= 0) | jnp.logical_not(first_span))
        )
        masked = jnp.where(valid, window_scores, -jnp.inf)
        highest_score = jnp.max(masked, axis=2, keepdims=True)
        expo = jnp.where(valid, jnp.exp(window_scores - highest_score), 0.0)
        weights = (expo / jnp.sum(expo, axis=2, keepdims=True)).astype(jnp.bfloat16)
        window_out = jnp.einsum(
            "hbc,chv->bhv", weights, value_window, preferred_element_type=jnp.float32
        )
        return (state, (intra + inter, window_out))

    final_state, (linear_all, window_all) = lax.scan(block_step, prefix, jnp.arange(block_count))
    linear = linear_all.reshape(span_rows, heads_here, VD)
    window = window_all.reshape(span_rows, heads_here, VD)
    scale = lax.rsqrt(jnp.mean(linear * linear, axis=2, keepdims=True) + epsilon)
    gains = gain.reshape(heads_here, VD)
    mixed = (linear * scale * gains + window).astype(jnp.bfloat16)
    tokens_back = lax.all_to_all(mixed, "head", split_axis=0, concat_axis=1, tiled=True)
    return tokens_back.reshape(tokens_back.shape[0], HEADS * VD)


def solution(mesh):
    placed = (
        P(("groups", "ctx", "head"), None),
        P(("groups", "ctx", "head"), None),
        P(("groups", "ctx", "head"), None),
        P("head"),
    )
    return jax.shard_map(
        per_device,
        mesh=mesh,
        in_specs=placed,
        out_specs=P(("groups", "ctx", "head"), None),
        check_vma=False,
    )
```

profile of v0, /device:TPU:0, one launch (start us, length us, event | category | flops | bytes accessed | tf_op | source)
XLA Modules:
  0.0 278.9 jit_solution(16457745592861958230)
XLA Ops:
  8.3 4.2 %all-to-all-start = ((bf16[256,32,16]{0,2,1:T(8,128)(2,1)}), bf16[256,32,16]{0,2,1:T(8,128)(2,1)S(1)}, u32[]{:S(2)}, u32[]{:S(2)}) async-start(bf16[256,32,16]{0,2,1:T(8,128)(2,1)} %bitcast.7), calls=%async_computation | async-start | bytes 524288 | tf_op jit(solution)/shard_map/all_to_all | solution.py:50
  18.7 3.6 %all-to-all-start.1 = ((bf16[256,32,128]{2,0,1:T(8,128)(2,1)}), bf16[256,32,128]{2,0,1:T(8,128)(2,1)S(1)}, u32[]{:S(2)}, u32[]{:S(2)}) async-start(bf16[256,32,128]{2,0,1:T(8,128)(2,1)} %copy.45), calls=%async_computation.1 | async-start | bytes 4194304 | tf_op jit(solution)/shard_map/all_to_all | solution.py:51
  23.8 3.9 %pad_maximum_fusion = bf16[1024,8,273]{0,2,1:T(8,128)(2,1)} fusion(bf16[1024,8,256]{0,2,1:T(8,128)(2,1)S(1)} %bitcast.76, bf16[1024,8,16]{0,2,1:T(8,128)(2,1)S(1)} %multiply_convert_fusion.3, bf16[273]{0:T(512)(128)(2,1)S(1)} %pad.7.clone), kind=kLoop, calls=%fused_computation.66 | loop fusion | flops 13418496 | bytes 8929826 | tf_op jit(solution)/shard_map/concatenate | solution.py:40
  27.7 20.3 %all-to-all-done.1 = bf16[256,32,128]{2,0,1:T(8,128)(2,1)S(1)} async-done(((bf16[256,32,128]{2,0,1:T(8,128)(2,1)}), bf16[256,32,128]{2,0,1:T(8,128)(2,1)S(1)}, u32[]{:S(2)}, u32[]{:S(2)}) %all-to-all-start.1) | async-done | bytes 2097184 | tf_op jit(solution)/shard_map/all_to_all | solution.py:51
  49.4 4.4 %fusion.77 = f32[8,273,128]{2,1,0:T(8,128)S(1)} fusion(bf16[1024,8,273]{0,2,1:T(8,128)(2,1)} %pad_maximum_fusion, bf16[1024,8,128]{2,0,1:T(8,128)(2,1)} %bitcast.15), kind=kOutput, calls=%fused_computation.77 | convolution fusion | flops 572522496 | bytes 7688192 | tf_op jit(solution)/shard_map/bhf,bhv->hfv/dot_general | solution.py:64
  55.9 3.4 %all-to-all-start.2 = ((bf16[256,32,16]{0,2,1:T(8,128)(2,1)}), bf16[256,32,16]{0,2,1:T(8,128)(2,1)S(1)}, u32[]{:S(2)}, u32[]{:S(2)}) async-start(bf16[256,32,16]{0,2,1:T(8,128)(2,1)} %bitcast.17), calls=%async_computation.2 | async-start | bytes 524288 | tf_op jit(solution)/shard_map/all_to_all | solution.py:49
  59.4 4.1 %collective-permute-start.1 = (bf16[64,8,16]{0,2,1:T(8,128)(2,1)S(1)}, bf16[64,8,16]{0,2,1:T(8,128)(2,1)S(1)}, u32[]{:S(2)}, u32[]{:S(2)}) collective-permute-start(bf16[64,8,16]{0,2,1:T(8,128)(2,1)S(1)} %slice.9), channel_id=1, source_target_pairs={{0,4},{4,8},{8,12},{1,5},{5,9},{9,13},{2,6},{6,10},{10,14},{3,7},{... | collective-permute-start | bytes 49160 | tf_op jit(solution)/shard_map/ppermute | solution.py:18
  67.0 4.3 %collective-permute-start = (bf16[64,8,128]{2,0,1:T(8,128)(2,1)S(1)}, bf16[64,8,128]{2,0,1:T(8,128)(2,1)S(1)}, u32[]{:S(2)}, u32[]{:S(2)}) collective-permute-start(bf16[64,8,128]{2,0,1:T(8,128)(2,1)S(1)} %slice.8), channel_id=1, source_target_pairs={{0,4},{4,8},{8,12},{1,5},{5,9},{9,13},{2,6},{6,10},{10,14},{3,7},{... | collective-permute-start | bytes 393224 | tf_op jit(solution)/shard_map/ppermute | solution.py:18
  72.2 5.1 %collective-permute-done = bf16[64,8,128]{2,0,1:T(8,128)(2,1)S(1)} collective-permute-done((bf16[64,8,128]{2,0,1:T(8,128)(2,1)S(1)}, bf16[64,8,128]{2,0,1:T(8,128)(2,1)S(1)}, u32[]{:S(2)}, u32[]{:S(2)}) %collective-permute-start) | collective-permute-done | bytes 131104 | tf_op jit(solution)/shard_map/ppermute | solution.py:18
  80.5 65.2 %all-gather.3.cloned.1.call-done = f32[32,273,128]{2,0,1:T(8,128)} async-done(((f32[8,273,128]{2,0,1:T(8,128)}), f32[32,273,128]{2,0,1:T(8,128)}) %all-gather.3.cloned.1.call-update) | async-done | bytes 4472848 | tf_op jit(solution)/shard_map/all_gather | solution.py:23
  145.7 7.5 %while.32 = (s32[]{:T(128)}, f32[8,273,128]{2,1,0:T(8,128)S(1)}, s32[]{:T(128)}, f32[4,8,273,128]{3,1,0,2:T(8,128)}, s32[]{:T(128)}, /*index=5*/s32[]{:T(128)}) while((s32[]{:T(128)}, f32[8,273,128]{2,1,0:T(8,128)S(1)}, s32[]{:T(128)}, f32[4,8,273,128]{3,1,0,2:T(8,128)}, s32[]{:T(128)}, /*index=5*/s32[]{:T(128)}) %tuple.69), condition=%wide.region_1.2_spmd.clone, body=%wide.region_0.1_spmd.clone.sunk | while | flops 838660 | bytes 5591141 | solution.py:31
  153.2 71.0 %while.31 = (s32[]{:T(128)}, f32[8,273,128]{2,1,0:T(8,128)S(1)}, f32[2,512,8,128]{1,3,2,0:T(8,128)}, f32[2,512,8,128]{3,2,1,0:T(8,128)}, s32[2]{0:T(128)S(1)}, /...) while((s32[]{:T(128)}, f32[8,273,128]{2,1,0:T(8,128)S(1)}, ...), condition=%wide.region_5.6_spmd, body=%wide.region_2.5_spmd.sunk | while | flops 1977677568 | bytes 70311560 | solution.py:120
  158.9 4.5 %fusion.111 = f32[8,128,512]{2,1,0:T(8,128)S(1)} fusion(pred[512,512]{1,0:T(8,128)(4,1)} %iota_compare_fusion.3, bf16[1024,8,128]{2,0,1:T(8,128)(2,1)} %get-tuple-element.495, s32[]{:T(128)S(6)} %select_n.84, bf16[1024,8,16]{0,2,1:T(8,128)(2,1)} %copy-done.1, bf16[1024,8,16]{0,2,1:T(8,128)(2,1)} %get-tuple-element.496), kind=kOutput, calls=%fused_computation.12.clone.1 | convolution fusion | flops 618659840 | bytes 3671552 | tf_op jit(solution)/shard_map/while/body/eval_jaxpr/hbc,chv->bhv/dot_general | solution.py:90
  164.2 3.7 %bitcast_dynamic-update-slice_fusion.2 = f32[2,512,8,128]{1,3,2,0:T(8,128)} fusion(f32[2,512,8,128]{1,3,2,0:T(8,128)} %get-tuple-element.472, s32[]{:T(128)S(6)} %copy.85, f32[8,128,512]{2,1,0:T(8,128)S(1)} %fusion.111, bf16[512,8,256]{0,2,1:T(8,128)(2,1)S(1)} %bitcast.73, bf16[512,8,16]{0,2,1:T(8,128)(2,1)} %multiply_convert_fusion.7, ...), kind=kOutput, calls=%fused_computation.22.clone.1 | convolution fusion | flops 293774336 | bytes 7541286 | tf_op jit(solution)/shard_map/while/body/eval_jaxpr/bhf,hfv->bhv/dot_general | solution.py:92
  170.2 8.4 %fusion.114 = (f32[8,512]{1,0:T(8,128)S(1)}, f32[8,512,576]{1,2,0:T(8,128)}) fusion(pred[512,576]{0,1:T(8,128)(4,1)S(1)} %copy-done, bf16[1088,8,16]{0,2,1:T(8,128)(2,1)S(1)} %copy-done.3, s32[]{:T(128)S(6)} %select_n.85, bf16[1024,8,16]{0,2,1:T(8,128)(2,1)} %get-tuple-element.496, s32[]{:T(128)S(6)} %select_n.84), kind=kOutput, calls=%fused_computation.76.clone.1 | convolution fusion | flops 165151296 | bytes 10635264 | tf_op jit(solution)/shard_map/while/body/eval_jaxpr/sub | solution.py:113
  178.6 6.5 %fusion.115 = f32[1,512,8,128]{1,3,2,0:T(8,128)} fusion(f32[8,512,576]{1,2,0:T(8,128)} %get-tuple-element.427, f32[8,512]{1,0:T(8,128)S(1)} %get-tuple-element.428, bf16[1088,8,128]{2,0,1:T(8,128)(2,1)} %get-tuple-element.498, s32[]{:T(128)S(6)} %select_n.85), kind=kOutput, calls=%fused_computation.24.clone.1 | convolution fusion | flops 608698368 | bytes 12730372 | tf_op jit(solution)/shard_map/while/body/eval_jaxpr/hbc,chv->bhv/dot_general | solution.py:115
  194.4 4.6 %fusion.111 = f32[8,128,512]{2,1,0:T(8,128)S(1)} fusion(pred[512,512]{1,0:T(8,128)(4,1)} %iota_compare_fusion.3, bf16[1024,8,128]{2,0,1:T(8,128)(2,1)} %get-tuple-element.495, s32[]{:T(128)S(6)} %select_n.84, bf16[1024,8,16]{0,2,1:T(8,128)(2,1)} %copy-done.1, bf16[1024,8,16]{0,2,1:T(8,128)(2,1)} %get-tuple-element.496), kind=kOutput, calls=%fused_computation.12.clone.1 | convolution fusion | flops 618659840 | bytes 3671552 | tf_op jit(solution)/shard_map/while/body/eval_jaxpr/hbc,chv->bhv/dot_general | solution.py:90
  199.6 3.7 %bitcast_dynamic-update-slice_fusion.2 = f32[2,512,8,128]{1,3,2,0:T(8,128)} fusion(f32[2,512,8,128]{1,3,2,0:T(8,128)} %get-tuple-element.472, s32[]{:T(128)S(6)} %copy.85, f32[8,128,512]{2,1,0:T(8,128)S(1)} %fusion.111, bf16[512,8,256]{0,2,1:T(8,128)(2,1)S(1)} %bitcast.73, bf16[512,8,16]{0,2,1:T(8,128)(2,1)} %multiply_convert_fusion.7, ...), kind=kOutput, calls=%fused_computation.22.clone.1 | convolution fusion | flops 293774336 | bytes 7541286 | tf_op jit(solution)/shard_map/while/body/eval_jaxpr/bhf,hfv->bhv/dot_general | solution.py:92
  205.7 8.4 %fusion.114 = (f32[8,512]{1,0:T(8,128)S(1)}, f32[8,512,576]{1,2,0:T(8,128)}) fusion(pred[512,576]{0,1:T(8,128)(4,1)S(1)} %copy-done, bf16[1088,8,16]{0,2,1:T(8,128)(2,1)S(1)} %copy-done.3, s32[]{:T(128)S(6)} %select_n.85, bf16[1024,8,16]{0,2,1:T(8,128)(2,1)} %get-tuple-element.496, s32[]{:T(128)S(6)} %select_n.84), kind=kOutput, calls=%fused_computation.76.clone.1 | convolution fusion | flops 165151296 | bytes 10635264 | tf_op jit(solution)/shard_map/while/body/eval_jaxpr/sub | solution.py:113
  214.1 6.5 %fusion.115 = f32[1,512,8,128]{1,3,2,0:T(8,128)} fusion(f32[8,512,576]{1,2,0:T(8,128)} %get-tuple-element.427, f32[8,512]{1,0:T(8,128)S(1)} %get-tuple-element.428, bf16[1088,8,128]{2,0,1:T(8,128)(2,1)} %get-tuple-element.498, s32[]{:T(128)S(6)} %select_n.85), kind=kOutput, calls=%fused_computation.24.clone.1 | convolution fusion | flops 608698368 | bytes 12730372 | tf_op jit(solution)/shard_map/while/body/eval_jaxpr/hbc,chv->bhv/dot_general | solution.py:115
  227.0 5.3 %copy.52 = f32[2,512,8,128]{3,2,1,0:T(8,128)} copy(f32[2,512,8,128]{1,3,2,0:T(8,128)} %get-tuple-element.272) | data formatting | bytes 8388608 | tf_op jit(solution)/shard_map/while | solution.py:120
  232.5 4.1 %fusion.66 = bf16[1024,8,128]{2,1,0:T(8,128)(2,1)S(1)} fusion(f32[2,512,8,128]{3,2,1,0:T(8,128)} %get-tuple-element.273, f32[2,512,8,128]{3,2,1,0:T(8,128)} %copy.52, f32[8,128]{1,0:T(8,128)S(1)} %bitcast.90, f32[1024,8]{1,0:T(8,128)S(1)} %copy.53), kind=kLoop, calls=%fused_computation.68 | loop fusion | flops 4194304 | bytes 10522624 | tf_op jit(solution)/shard_map/convert_element_type | solution.py:125
  236.6 28.8 %all_to_all.69 = bf16[1024,8,128]{2,1,0:T(8,128)(2,1)S(1)} all-to-all(bf16[1024,8,128]{2,1,0:T(8,128)(2,1)S(1)} %fusion.66), channel_id=1, replica_groups=mesh['groups'=2,'ctx'=4,'head'=4] {'head'}, dimensions={0} | all-to-all | bytes 4194304 | tf_op jit(solution)/shard_map/all_to_all | solution.py:126
  268.0 4.1 %copy.56 = bf16[256,4096]{1,0:T(8,128)(2,1)} copy(bf16[256,4096]{0,1:T(8,128)(2,1)} %bitcast.79) | data formatting | bytes 4194304 | tf_op jit(solution)/shard_map/reshape | solution.py:127
  (93 shorter events, 56.7 us)
Async XLA Ops:
  8.3 10.3 %all-to-all-start = ((bf16[256,32,16]{0,2,1:T(8,128)(2,1)}), bf16[256,32,16]{0,2,1:T(8,128)(2,1)S(1)}, u32[]{:S(2)}, u32[]{:S(2)}) async-start(bf16[256,32,16]{0,2,1:T(8,128)(2,1)} %bitcast.7), calls=%async_computation | async-start | bytes 524288 | tf_op jit(solution)/shard_map/all_to_all | solution.py:50
  18.7 29.3 %all-to-all-start.1 = ((bf16[256,32,128]{2,0,1:T(8,128)(2,1)}), bf16[256,32,128]{2,0,1:T(8,128)(2,1)S(1)}, u32[]{:S(2)}, u32[]{:S(2)}) async-start(bf16[256,32,128]{2,0,1:T(8,128)(2,1)} %copy.45), calls=%async_computation.1 | async-start | bytes 4194304 | tf_op jit(solution)/shard_map/all_to_all | solution.py:51
  22.3 123.4 %all-gather.3.cloned.1.call-start = ((), (), s32[]{:S(2)}) async-start(), calls=%async_computation.4 | async-start | bytes 5591040 | tf_op jit(solution)/shard_map/all_gather | solution.py:23
  49.4 5.7 %copy-start.4 = (bf16[256,512]{1,0:T(8,128)(2,1)S(1)}, bf16[256,512]{1,0:T(8,128)(2,1)}, u32[]{:S(2)}) copy-start(bf16[256,512]{1,0:T(8,128)(2,1)} %param.8) | copy-start | bytes 786436
  55.9 9.4 %all-to-all-start.2 = ((bf16[256,32,16]{0,2,1:T(8,128)(2,1)}), bf16[256,32,16]{0,2,1:T(8,128)(2,1)S(1)}, u32[]{:S(2)}, u32[]{:S(2)}) async-start(bf16[256,32,16]{0,2,1:T(8,128)(2,1)} %bitcast.17), calls=%async_computation.2 | async-start | bytes 524288 | tf_op jit(solution)/shard_map/all_to_all | solution.py:49
  59.4 11.9 %collective-permute-start.1 = (bf16[64,8,16]{0,2,1:T(8,128)(2,1)S(1)}, bf16[64,8,16]{0,2,1:T(8,128)(2,1)S(1)}, u32[]{:S(2)}, u32[]{:S(2)}) collective-permute-start(bf16[64,8,16]{0,2,1:T(8,128)(2,1)S(1)} %slice.9), channel_id=1, source_target_pairs={{0,4},{4,8},{8,12},{1,5},{5,9},{9,13},{2,6},{6,10},{10,14},{3,7},{... | collective-permute-start | bytes 49160 | tf_op jit(solution)/shard_map/ppermute | solution.py:18
  67.0 10.3 %collective-permute-start = (bf16[64,8,128]{2,0,1:T(8,128)(2,1)S(1)}, bf16[64,8,128]{2,0,1:T(8,128)(2,1)S(1)}, u32[]{:S(2)}, u32[]{:S(2)}) collective-permute-start(bf16[64,8,128]{2,0,1:T(8,128)(2,1)S(1)} %slice.8), channel_id=1, source_target_pairs={{0,4},{4,8},{8,12},{1,5},{5,9},{9,13},{2,6},{6,10},{10,14},{3,7},{... | collective-permute-start | bytes 393224 | tf_op jit(solution)/shard_map/ppermute | solution.py:18
  153.2 4.6 %copy-start.1 = (bf16[1024,8,16]{0,2,1:T(8,128)(2,1)}, bf16[1024,8,16]{0,2,1:T(8,128)(2,1)S(1)}, u32[]{:S(2)}) copy-start(bf16[1024,8,16]{0,2,1:T(8,128)(2,1)S(1)} %get-tuple-element.497) | copy-start | bytes 786436 | tf_op jit(solution)/shard_map/while
  163.5 4.4 %slice-start = ((s8[4587520]{0:T(1024)(128)(4,1)}), s8[4194304]{0:T(1024)(128)(4,1)S(1)}, s32[]{:S(2)}) async-start(s8[4587520]{0:T(1024)(128)(4,1)} %bitcast.74), calls=%async_computation.5 | async-start | bytes 8388608 | tf_op jit(solution)/shard_map/while
  164.2 3.7 %slice-start.1 = ((s8[4587520]{0:T(1024)(128)(4,1)}), s8[393216]{0:T(1024)(128)(4,1)S(1)}, s32[]{:S(2)}) async-start(s8[4587520]{0:T(1024)(128)(4,1)} %bitcast.74), calls=%async_computation.6 | async-start | bytes 786432 | tf_op jit(solution)/shard_map/while
  167.9 2.3 copy-start
  167.9 2.3 copy-start.3
  185.1 3.6 %copy-start.2 = (bf16[1024,8,16]{0,2,1:T(8,128)(2,1)S(1)}, bf16[1024,8,16]{0,2,1:T(8,128)(2,1)}, u32[]{:S(2)}) copy-start(bf16[1024,8,16]{0,2,1:T(8,128)(2,1)} %copy-done.1) | copy-start | bytes 786436 | tf_op jit(solution)/shard_map/while
  188.7 4.6 %copy-start.1 = (bf16[1024,8,16]{0,2,1:T(8,128)(2,1)}, bf16[1024,8,16]{0,2,1:T(8,128)(2,1)S(1)}, u32[]{:S(2)}) copy-start(bf16[1024,8,16]{0,2,1:T(8,128)(2,1)S(1)} %get-tuple-element.497) | copy-start | bytes 786436 | tf_op jit(solution)/shard_map/while
  198.9 4.4 %slice-start = ((s8[4587520]{0:T(1024)(128)(4,1)}), s8[4194304]{0:T(1024)(128)(4,1)S(1)}, s32[]{:S(2)}) async-start(s8[4587520]{0:T(1024)(128)(4,1)} %bitcast.74), calls=%async_computation.5 | async-start | bytes 8388608 | tf_op jit(solution)/shard_map/while
  199.6 3.7 %slice-start.1 = ((s8[4587520]{0:T(1024)(128)(4,1)}), s8[393216]{0:T(1024)(128)(4,1)S(1)}, s32[]{:S(2)}) async-start(s8[4587520]{0:T(1024)(128)(4,1)} %bitcast.74), calls=%async_computation.6 | async-start | bytes 786432 | tf_op jit(solution)/shard_map/while
  203.4 2.4 copy-start
  203.4 2.4 copy-start.3
  220.6 3.6 %copy-start.2 = (bf16[1024,8,16]{0,2,1:T(8,128)(2,1)S(1)}, bf16[1024,8,16]{0,2,1:T(8,128)(2,1)}, u32[]{:S(2)}) copy-start(bf16[1024,8,16]{0,2,1:T(8,128)(2,1)} %copy-done.1) | copy-start | bytes 786436 | tf_op jit(solution)/shard_map/while
  227.0 5.5 %copy-start.5 = (f32[1024]{0:T(1024)S(1)}, f32[1024]{0:T(1024)}, u32[]{:S(2)}) copy-start(f32[1024]{0:T(1024)} %param.11) | copy-start | bytes 12292
Sparse Core Ops, SparseCore 0:
  55.2 90.4 all-gather.2
where the time goes:
time: 280 us; the launch traced here: 279 us
  waiting for transfers between devices  92.4 us (33%)
  matrix products  55.3 us (20%)
  local copies, waits for them, and re-layouts  39.3 us (14%)
  blocking collectives  28.8 us (10%)
  other arithmetic  28.4 us (10%)
  starting transfers between devices  19.7 us (7%)
  between operations  13.6 us (5%)
    all_gather x1, waiting for transfers between devices, entering(): everything = lax.all_gather(shard, axis)  65.2 us
    all_to_all x1, blocking collectives, per_device(): lax.all_to_all(mixed, 'head', split_axis=0, concat_axis=1, tiled=True)  28.8 us
    all_to_all x1, waiting for transfers between devices, per_device(): lax.all_to_all(value_tok, 'head', split_axis=1, concat_axis=0, tiled=True)  20.3 us
    sub x2, matrix products, block_step(): expo = jnp.where(valid, jnp.exp(window_scores - highest_score), 0.0)  16.7 us
    dot_general x2, matrix products, block_step(): jnp.einsum('hbc,chv->bhv', weights, value_window, preferred_element_type=...  13 us
    dot_general x2, matrix products, block_step(): jnp.einsum('hbc,chv->bhv', kernel, value_block, preferred_element_type=jn...  9.1 us
    ppermute x2, starting transfers between devices, shifted(): return lax.ppermute(shard, axis, pairs)  8.46 us
    dot_general x2, matrix products, block_step(): jnp.einsum('bhf,hfv->bhv', query_feat, state.astype(jnp.bfloat16), prefer...  7.45 us
  transfers between devices with their start and end apart: 6, of which 4 were waited for; matrix products, arithmetic and copies ran while one was open for 6% of the time, Pallas kernels for 0%

commit v1 on v0

--- a/solution.py
+++ b/solution.py
@@ -10,6 +10,17 @@
 WINDOW = 64
 outer_scale = 1.0 / (4.0 * math.sqrt(2.0))
 epsilon = 1e-06
+
+
+def split_up(x, dim, length):
+    before, after = (x.shape[:dim], x.shape[dim + 1 :])
+    return jnp.moveaxis(x.reshape(*before, length, -1, *after), dim, 0)
+
+
+def joined_along(blocks, dim):
+    blocks = jnp.moveaxis(blocks, 0, dim)
+    dims = blocks.shape
+    return blocks.reshape(*dims[:dim], dims[dim] * dims[dim + 1], *dims[dim + 2 :])
 
 
 def shifted(shard, axis, by):
@@ -123,7 +134,14 @@
     scale = lax.rsqrt(jnp.mean(linear * linear, axis=2, keepdims=True) + epsilon)
     gains = gain.reshape(heads_here, VD)
     mixed = (linear * scale * gains + window).astype(jnp.bfloat16)
-    tokens_back = lax.all_to_all(mixed, "head", split_axis=0, concat_axis=1, tiled=True)
+    count, index = (lax.axis_size("head"), lax.axis_index("head"))
+    pieces = split_up(mixed, 0, count)
+    done = [pieces[index]]
+    for step in range(1, count):
+        sent = pieces[index ^ step]
+        done.append(lax.ppermute(sent, "head", [(i_2, i_2 ^ step) for i_2 in range(count)]))
+    pieces = jnp.stack(done)[index ^ jnp.arange(count)]
+    tokens_back = joined_along(pieces, 1)
     return tokens_back.reshape(tokens_back.shape[0], HEADS * VD)
 
 

time: 280 us -> 262 us (0.936)
  blocking collectives: 28.8 us -> 0 us
  waiting for transfers between devices: 92.4 us -> 111 us
  matrix products: 55.3 us -> 48.4 us
  other arithmetic: 28.4 us -> 21.8 us
    all_to_all x1 -> x0, blocking collectives: 28.8 us -> none  [per_device(): lax.all_to_all(mixed, 'head', split_axis=0, concat_axis=1, tiled=True)]
    ppermute x0 -> x3, waiting for transfers between devices: none -> 23.2 us  [per_device(): lax.ppermute(sent, 'head', [(i_2, i_2 ^ step) for i_2 in range(count)])]
    reshape x1 -> x0, local copies, waits for them, and re-layouts: 4.06 us -> none  [per_device(): return tokens_back.reshape(tokens_back.shape[0], HEADS * VD)]
    transpose x0 -> x1, local copies, waits for them, and re-layouts: none -> 2.99 us  [joined_along(): blocks = jnp.moveaxis(blocks, 0, dim)]
    another operation x0 -> x1, local copies, waits for them, and re-layouts: none -> 2.86 us  [per_device(): return tokens_back.reshape(tokens_back.shape[0], HEADS * VD)]
    all_gather x1, waiting for transfers between devices: 65.2 us -> 62.4 us  [entering(): everything = lax.all_gather(shard, axis)]
    another operation x8 -> x9, other arithmetic: 5.83 us -> 3.05 us
    unnamed x7 -> x15, local copies, waits for them, and re-layouts: 5.9 us -> 7.22 us
  transfers between devices with their start and end apart: 6 -> 9, of which waited for: 4 -> 6; matrix products, arithmetic and copies ran while one was open for 6% -> 7% of each run, Pallas kernels for 0% -> 0%
where the time goes in v1:
time: 262 us; the launch traced here: 261 us
  waiting for transfers between devices  111 us (42%)
  matrix products  48.4 us (18%)
  local copies, waits for them, and re-layouts  42 us (16%)
  starting transfers between devices  22.3 us (9%)
  other arithmetic  21.8 us (8%)
  between operations  13.7 us (5%)
    all_gather x1, waiting for transfers between devices, entering(): everything = lax.all_gather(shard, axis)  62.4 us
    ppermute x3, waiting for transfers between devices, per_device(): lax.ppermute(sent, 'head', [(i_2, i_2 ^ step) for i_2 in range(count)])  23.2 us
    all_to_all x1, waiting for transfers between devices, per_device(): lax.all_to_all(value_tok, 'head', split_axis=1, concat_axis=0, tiled=True)  20.3 us
    sub x2, matrix products, block_step(): expo = jnp.where(valid, jnp.exp(window_scores - highest_score), 0.0)  14.9 us
    dot_general x2, matrix products, block_step(): jnp.einsum('hbc,chv->bhv', weights, value_window, preferred_element_type=...  13 us
    dot_general x2, matrix products, block_step(): jnp.einsum('hbc,chv->bhv', kernel, value_block, preferred_element_type=jn...  9.02 us
    ppermute x2, starting transfers between devices, shifted(): return lax.ppermute(shard, axis, pairs)  8.45 us
    unnamed x15, local copies, waits for them, and re-layouts  7.22 us
  transfers between devices with their start and end apart: 9, of which 6 were waited for; matrix products, arithmetic and copies ran while one was open for 7% of the time, Pallas kernels for 0%

profile of v1, /device:TPU:0, one launch (start us, length us, event | category | flops | bytes accessed | tf_op | source)
XLA Modules:
  0.0 260.9 jit_solution(7984980481549236115)
XLA Ops:
  8.3 4.2 %all-to-all-start = ((bf16[256,32,16]{0,2,1:T(8,128)(2,1)}), bf16[256,32,16]{0,2,1:T(8,128)(2,1)S(1)}, u32[]{:S(2)}, u32[]{:S(2)}) async-start(bf16[256,32,16]{0,2,1:T(8,128)(2,1)} %bitcast.7), calls=%async_computation | async-start | bytes 524288 | tf_op jit(solution)/shard_map/all_to_all | solution.py:61
  12.5 3.3 %copy.44 = bf16[256,4096]{0,1:T(8,128)(2,1)S(1)} copy(bf16[256,4096]{1,0:T(8,128)(2,1)} %param.10) | data formatting | bytes 4194304 | tf_op args[2]
  18.7 3.6 %all-to-all-start.1 = ((bf16[256,32,128]{2,0,1:T(8,128)(2,1)}), bf16[256,32,128]{2,0,1:T(8,128)(2,1)S(1)}, u32[]{:S(2)}, u32[]{:S(2)}) async-start(bf16[256,32,128]{2,0,1:T(8,128)(2,1)} %copy.45), calls=%async_computation.1 | async-start | bytes 4194304 | tf_op jit(solution)/shard_map/all_to_all | solution.py:62
  23.9 3.8 %pad_maximum_fusion = bf16[1024,8,273]{0,2,1:T(8,128)(2,1)} fusion(bf16[1024,8,256]{0,2,1:T(8,128)(2,1)S(1)} %bitcast.82, bf16[1024,8,16]{0,2,1:T(8,128)(2,1)S(1)} %multiply_convert_fusion.3, bf16[273]{0:T(512)(128)(2,1)S(1)} %pad.11.clone), kind=kLoop, calls=%fused_computation.67 | loop fusion | flops 13418496 | bytes 8929826 | tf_op jit(solution)/shard_map/concatenate | solution.py:51
  27.7 20.3 %all-to-all-done.1 = bf16[256,32,128]{2,0,1:T(8,128)(2,1)S(1)} async-done(((bf16[256,32,128]{2,0,1:T(8,128)(2,1)}), bf16[256,32,128]{2,0,1:T(8,128)(2,1)S(1)}, u32[]{:S(2)}, u32[]{:S(2)}) %all-to-all-start.1) | async-done | bytes 2097184 | tf_op jit(solution)/shard_map/all_to_all | solution.py:62
  51.0 4.4 %fusion.76 = f32[8,273,128]{2,1,0:T(8,128)S(1)} fusion(bf16[1024,8,273]{0,2,1:T(8,128)(2,1)} %pad_maximum_fusion, bf16[1024,8,128]{2,0,1:T(8,128)(2,1)S(1)} %bitcast.77), kind=kOutput, calls=%fused_computation.83 | convolution fusion | flops 572522496 | bytes 7688192 | tf_op jit(solution)/shard_map/bhf,bhv->hfv/dot_general | solution.py:75
  57.6 4.0 %all-to-all-start.2 = ((bf16[256,32,16]{0,2,1:T(8,128)(2,1)}), bf16[256,32,16]{0,2,1:T(8,128)(2,1)}, u32[]{:S(2)}, u32[]{:S(2)}) async-start(bf16[256,32,16]{0,2,1:T(8,128)(2,1)} %bitcast.17), calls=%async_computation.2 | async-start | bytes 524288 | tf_op jit(solution)/shard_map/all_to_all | solution.py:60
  62.3 4.1 %collective-permute-start.1 = (bf16[64,8,16]{0,2,1:T(8,128)(2,1)}, bf16[64,8,16]{0,2,1:T(8,128)(2,1)S(1)}, u32[]{:S(2)}, u32[]{:S(2)}) collective-permute-start(bf16[64,8,16]{0,2,1:T(8,128)(2,1)} %slice.11), channel_id=1, source_target_pairs={{0,4},{4,8},{8,12},{1,5},{5,9},{9,13},{2,6},{6,10},{10,14},{3,7},{... | collective-permute-start | bytes 49160 | tf_op jit(solution)/shard_map/ppermute | solution.py:29
  68.7 4.3 %collective-permute-start = (bf16[64,8,128]{2,0,1:T(8,128)(2,1)S(1)}, bf16[64,8,128]{2,0,1:T(8,128)(2,1)S(1)}, u32[]{:S(2)}, u32[]{:S(2)}) collective-permute-start(bf16[64,8,128]{2,0,1:T(8,128)(2,1)S(1)} %slice.10), channel_id=1, source_target_pairs={{0,4},{4,8},{8,12},{1,5},{5,9},{9,13},{2,6},{6,10},{10,14},{3,7},{... | collective-permute-start | bytes 393224 | tf_op jit(solution)/shard_map/ppermute | solution.py:29
  74.9 4.2 %collective-permute-done = bf16[64,8,128]{2,0,1:T(8,128)(2,1)S(1)} collective-permute-done((bf16[64,8,128]{2,0,1:T(8,128)(2,1)S(1)}, bf16[64,8,128]{2,0,1:T(8,128)(2,1)S(1)}, u32[]{:S(2)}, u32[]{:S(2)}) %collective-permute-start) | collective-permute-done | bytes 131104 | tf_op jit(solution)/shard_map/ppermute | solution.py:29
  80.6 62.4 %all-gather.3.cloned.1.call-done = f32[32,273,128]{2,0,1:T(8,128)} async-done(((f32[8,273,128]{2,0,1:T(8,128)}), f32[32,273,128]{2,0,1:T(8,128)}) %all-gather.3.cloned.1.call-update) | async-done | bytes 4472848 | tf_op jit(solution)/shard_map/all_gather | solution.py:34
  142.9 7.6 %while.32 = (s32[]{:T(128)}, f32[8,273,128]{2,1,0:T(8,128)S(1)}, s32[]{:T(128)}, f32[4,8,273,128]{3,1,0,2:T(8,128)}, s32[]{:T(128)}, /*index=5*/s32[]{:T(128)}) while((s32[]{:T(128)}, f32[8,273,128]{2,1,0:T(8,128)S(1)}, s32[]{:T(128)}, f32[4,8,273,128]{3,1,0,2:T(8,128)}, s32[]{:T(128)}, /*index=5*/s32[]{:T(128)}) %tuple.74), condition=%wide.region_1.2_spmd.clone, body=%wide.region_0.1_spmd.clone.sunk | while | flops 838660 | bytes 5591133 | solution.py:42
  150.5 57.5 %while.31 = (s32[]{:T(128)}, f32[8,273,128]{2,1,0:T(8,128)S(1)}, f32[2,512,8,128]{1,3,2,0:T(8,128)}, f32[2,512,8,128]{3,2,1,0:T(8,128)}, s32[2]{0:T(128)S(1)}, /...) while((s32[]{:T(128)}, f32[8,273,128]{2,1,0:T(8,128)S(1)}, ...), condition=%wide.region_5.6_spmd, body=%wide.region_2.5_spmd.sunk | while | flops 1977677568 | bytes 75424320 | solution.py:131
  152.1 7.4 %fusion.113 = (f32[8,512]{1,0:T(8,128)S(1)}, f32[8,512,576]{1,2,0:T(8,128)}) fusion(pred[512,576]{0,1:T(8,128)(4,1)S(1)} %fusion.112, bf16[1088,8,16]{0,2,1:T(8,128)(2,1)S(1)} %get-tuple-element.504, s32[]{:T(128)S(6)} %select_n.115, bf16[1024,8,16]{0,2,1:T(8,128)(2,1)S(1)} %get-tuple-element.500, s32[]{:T(128)S(6)} %select_n.114), kind=kOutput, calls=%fused_computation.82.clone.1 | convolution fusion | flops 165151296 | bytes 10635264 | tf_op jit(solution)/shard_map/while/body/eval_jaxpr/sub | solution.py:124
  159.5 6.5 %fusion.114 = f32[1,512,8,128]{1,3,2,0:T(8,128)} fusion(f32[8,512,576]{1,2,0:T(8,128)} %get-tuple-element.431, f32[8,512]{1,0:T(8,128)S(1)} %get-tuple-element.432, bf16[1088,8,128]{2,0,1:T(8,128)(2,1)} %get-tuple-element.502, s32[]{:T(128)S(6)} %select_n.115), kind=kOutput, calls=%fused_computation.25.clone.1 | convolution fusion | flops 608698368 | bytes 12730372 | tf_op jit(solution)/shard_map/while/body/eval_jaxpr/hbc,chv->bhv/dot_general | solution.py:126
  170.4 4.5 %fusion.110 = f32[8,128,512]{2,1,0:T(8,128)S(1)} fusion(pred[512,512]{1,0:T(8,128)(4,1)} %iota_compare_fusion.3, bf16[1024,8,128]{2,0,1:T(8,128)(2,1)} %get-tuple-element.499, s32[]{:T(128)S(6)} %select_n.114, bf16[1024,8,16]{0,2,1:T(8,128)(2,1)} %get-tuple-element.501, bf16[1024,8,16]{0,2,1:T(8,128)(2,1)S(1)} %get-tuple-element.500), kind=kOutput, calls=%fused_computation.13.clone.1 | convolution fusion | flops 618659840 | bytes 3671552 | tf_op jit(solution)/shard_map/while/body/eval_jaxpr/hbc,chv->bhv/dot_general | solution.py:101
  180.8 7.4 %fusion.113 = (f32[8,512]{1,0:T(8,128)S(1)}, f32[8,512,576]{1,2,0:T(8,128)}) fusion(pred[512,576]{0,1:T(8,128)(4,1)S(1)} %fusion.112, bf16[1088,8,16]{0,2,1:T(8,128)(2,1)S(1)} %get-tuple-element.504, s32[]{:T(128)S(6)} %select_n.115, bf16[1024,8,16]{0,2,1:T(8,128)(2,1)S(1)} %get-tuple-element.500, s32[]{:T(128)S(6)} %select_n.114), kind=kOutput, calls=%fused_computation.82.clone.1 | convolution fusion | flops 165151296 | bytes 10635264 | tf_op jit(solution)/shard_map/while/body/eval_jaxpr/sub | solution.py:124
  188.2 6.5 %fusion.114 = f32[1,512,8,128]{1,3,2,0:T(8,128)} fusion(f32[8,512,576]{1,2,0:T(8,128)} %get-tuple-element.431, f32[8,512]{1,0:T(8,128)S(1)} %get-tuple-element.432, bf16[1088,8,128]{2,0,1:T(8,128)(2,1)} %get-tuple-element.502, s32[]{:T(128)S(6)} %select_n.115), kind=kOutput, calls=%fused_computation.25.clone.1 | convolution fusion | flops 608698368 | bytes 12730372 | tf_op jit(solution)/shard_map/while/body/eval_jaxpr/hbc,chv->bhv/dot_general | solution.py:126
  199.2 4.5 %fusion.110 = f32[8,128,512]{2,1,0:T(8,128)S(1)} fusion(pred[512,512]{1,0:T(8,128)(4,1)} %iota_compare_fusion.3, bf16[1024,8,128]{2,0,1:T(8,128)(2,1)} %get-tuple-element.499, s32[]{:T(128)S(6)} %select_n.114, bf16[1024,8,16]{0,2,1:T(8,128)(2,1)} %get-tuple-element.501, bf16[1024,8,16]{0,2,1:T(8,128)(2,1)S(1)} %get-tuple-element.500), kind=kOutput, calls=%fused_computation.13.clone.1 | convolution fusion | flops 618659840 | bytes 3671552 | tf_op jit(solution)/shard_map/while/body/eval_jaxpr/hbc,chv->bhv/dot_general | solution.py:101
  208.1 5.3 %copy.52 = f32[2,512,8,128]{3,2,1,0:T(8,128)} copy(f32[2,512,8,128]{1,3,2,0:T(8,128)} %get-tuple-element.526) | data formatting | bytes 8388608 | tf_op jit(solution)/shard_map/while | solution.py:131
  216.3 4.1 %add_convert_fusion = bf16[4,256,8,128]{3,2,1,0:T(8,128)(2,1)S(1)} fusion(f32[4,256,8,128]{3,2,1,0:T(8,128)} %bitcast.94, f32[4,256,8,128]{3,2,1,0:T(8,128)} %bitcast.81, f32[8,128]{1,0:T(8,128)S(1)} %bitcast.100, f32[4,256,8]{2,1,0:T(8,128)S(1)} %copy.53), kind=kLoop, calls=%fused_computation.68 | loop fusion | flops 4194304 | bytes 10522624 | tf_op jit(solution)/shard_map/convert_element_type | solution.py:136
  222.6 12.9 %collective-permute-done.3 = bf16[256,8,128]{2,1,0:T(8,128)(2,1)S(1)} collective-permute-done((bf16[256,8,128]{2,1,0:T(8,128)(2,1)S(1)}, bf16[256,8,128]{2,1,0:T(8,128)(2,1)S(1)}, u32[]{:S(2)}, u32[]{:S(2)}) %collective-permute-start.3) | collective-permute-done | bytes 524320 | tf_op jit(solution)/shard_map/ppermute | solution.py:142
  235.5 10.3 %collective-permute-done.4 = bf16[256,8,128]{2,1,0:T(8,128)(2,1)S(1)} collective-permute-done((bf16[256,8,128]{2,1,0:T(8,128)(2,1)S(1)}, bf16[256,8,128]{2,1,0:T(8,128)(2,1)S(1)}, u32[]{:S(2)}, u32[]{:S(2)}) %collective-permute-start.4) | collective-permute-done | bytes 524320 | tf_op jit(solution)/shard_map/ppermute | solution.py:142
  248.2 3.0 %copy.55 = bf16[256,4,8,128]{0,3,2,1:T(8,128)(2,1)S(1)} copy(bf16[256,4,8,128]{3,2,0,1:T(8,128)(2,1)} %bitcast.85) | data formatting | bytes 4194304 | tf_op jit(solution)/shard_map/transpose | solution.py:21
  (103 shorter events, 54.6 us)
Async XLA Ops:
  8.3 10.3 %all-to-all-start = ((bf16[256,32,16]{0,2,1:T(8,128)(2,1)}), bf16[256,32,16]{0,2,1:T(8,128)(2,1)S(1)}, u32[]{:S(2)}, u32[]{:S(2)}) async-start(bf16[256,32,16]{0,2,1:T(8,128)(2,1)} %bitcast.7), calls=%async_computation | async-start | bytes 524288 | tf_op jit(solution)/shard_map/all_to_all | solution.py:61
  18.7 29.3 %all-to-all-start.1 = ((bf16[256,32,128]{2,0,1:T(8,128)(2,1)}), bf16[256,32,128]{2,0,1:T(8,128)(2,1)S(1)}, u32[]{:S(2)}, u32[]{:S(2)}) async-start(bf16[256,32,128]{2,0,1:T(8,128)(2,1)} %copy.45), calls=%async_computation.1 | async-start | bytes 4194304 | tf_op jit(solution)/shard_map/all_to_all | solution.py:62
  22.3 120.6 %all-gather.3.cloned.1.call-start = ((), (), s32[]{:S(2)}) async-start(), calls=%async_computation.3 | async-start | bytes 5591040 | tf_op jit(solution)/shard_map/all_gather | solution.py:34
  22.4 39.2 %copy-start.3 = (bf16[4,8,2,8,256]{4,3,0,2,1:T(8,128)(2,1)}, bf16[4,8,2,8,256]{4,3,0,2,1:T(8,128)(2,1)S(1)}, u32[]{:S(2)}) copy-start(bf16[4,8,2,8,256]{4,3,0,2,1:T(8,128)(2,1)S(1)} %copy.64) | copy-start | bytes 786436
  48.0 1.3 copy-start.2
  51.0 28.0 %copy-start = (bf16[4,256,8,128]{3,1,0,2:T(8,128)(2,1)}, bf16[4,256,8,128]{3,1,0,2:T(8,128)(2,1)S(1)}, u32[]{:S(2)}) copy-start(bf16[4,256,8,128]{3,1,0,2:T(8,128)(2,1)S(1)} %copy.47) | copy-start | bytes 6291460
  51.0 5.7 %copy-start.6 = (bf16[256,512]{1,0:T(8,128)(2,1)S(1)}, bf16[256,512]{1,0:T(8,128)(2,1)}, u32[]{:S(2)}) copy-start(bf16[256,512]{1,0:T(8,128)(2,1)} %param.8) | copy-start | bytes 786436
  57.6 10.1 %all-to-all-start.2 = ((bf16[256,32,16]{0,2,1:T(8,128)(2,1)}), bf16[256,32,16]{0,2,1:T(8,128)(2,1)}, u32[]{:S(2)}, u32[]{:S(2)}) async-start(bf16[256,32,16]{0,2,1:T(8,128)(2,1)} %bitcast.17), calls=%async_computation.2 | async-start | bytes 524288 | tf_op jit(solution)/shard_map/all_to_all | solution.py:60
  62.3 10.7 %collective-permute-start.1 = (bf16[64,8,16]{0,2,1:T(8,128)(2,1)}, bf16[64,8,16]{0,2,1:T(8,128)(2,1)S(1)}, u32[]{:S(2)}, u32[]{:S(2)}) collective-permute-start(bf16[64,8,16]{0,2,1:T(8,128)(2,1)} %slice.11), channel_id=1, source_target_pairs={{0,4},{4,8},{8,12},{1,5},{5,9},{9,13},{2,6},{6,10},{10,14},{3,7},{... | collective-permute-start | bytes 49160 | tf_op jit(solution)/shard_map/ppermute | solution.py:29
  68.7 10.3 %collective-permute-start = (bf16[64,8,128]{2,0,1:T(8,128)(2,1)S(1)}, bf16[64,8,128]{2,0,1:T(8,128)(2,1)S(1)}, u32[]{:S(2)}, u32[]{:S(2)}) collective-permute-start(bf16[64,8,128]{2,0,1:T(8,128)(2,1)S(1)} %slice.10), channel_id=1, source_target_pairs={{0,4},{4,8},{8,12},{1,5},{5,9},{9,13},{2,6},{6,10},{10,14},{3,7},{... | collective-permute-start | bytes 393224 | tf_op jit(solution)/shard_map/ppermute | solution.py:29
  142.9 7.6 %copy-start.4 = (bf16[1088,8,16]{0,2,1:T(8,128)(2,1)S(1)}, bf16[1088,8,16]{0,2,1:T(8,128)(2,1)}, u32[]{:S(2)}) copy-start(bf16[1088,8,16]{0,2,1:T(8,128)(2,1)} %pad_maximum_fusion.3) | copy-start | bytes 835588
  175.0 3.3 %slice-start = ((s8[4587520]{0:T(1024)(128)(4,1)}), s8[4194304]{0:T(1024)(128)(4,1)S(1)}, s32[]{:S(2)}) async-start(s8[4587520]{0:T(1024)(128)(4,1)} %bitcast.75), calls=%async_computation.4 | async-start | bytes 8388608 | tf_op jit(solution)/shard_map/while
  175.7 2.6 copy-start.1
  175.7 2.5 slice-start.1
  178.2 1.0 copy-start.5
  203.7 3.3 %slice-start = ((s8[4587520]{0:T(1024)(128)(4,1)}), s8[4194304]{0:T(1024)(128)(4,1)S(1)}, s32[]{:S(2)}) async-start(s8[4587520]{0:T(1024)(128)(4,1)} %bitcast.75), calls=%async_computation.4 | async-start | bytes 8388608 | tf_op jit(solution)/shard_map/while
  204.4 2.6 copy-start.1
  204.5 2.5 slice-start.1
  207.0 1.1 copy-start.5
  213.3 3.0 %copy-start.7 = (f32[1024]{0:T(1024)S(1)}, f32[1024]{0:T(1024)}, u32[]{:S(2)}) copy-start(f32[1024]{0:T(1024)} %param.11) | copy-start | bytes 12292
  220.6 2.0 collective-permute-start.2
  220.7 14.8 %collective-permute-start.3 = (bf16[256,8,128]{2,1,0:T(8,128)(2,1)S(1)}, bf16[256,8,128]{2,1,0:T(8,128)(2,1)S(1)}, u32[]{:S(2)}, u32[]{:S(2)}) collective-permute-start(bf16[256,8,128]{2,1,0:T(8,128)(2,1)S(1)} %get-tuple-element.333), channel_id=1, source_target_pairs={{0,2},{1,3},{2,0},{3,1},{4,6},{5,7},{6,4},{7,5},{8,10},{9,11},{10,... | collective-permute-start | bytes 1572872 | tf_op jit(solution)/shard_map/ppermute | solution.py:142
  222.2 23.6 %collective-permute-start.4 = (bf16[256,8,128]{2,1,0:T(8,128)(2,1)S(1)}, bf16[256,8,128]{2,1,0:T(8,128)(2,1)S(1)}, u32[]{:S(2)}, u32[]{:S(2)}) collective-permute-start(bf16[256,8,128]{2,1,0:T(8,128)(2,1)S(1)} %get-tuple-element.332), channel_id=1, source_target_pairs={{0,3},{1,2},{2,1},{3,0},{4,7},{5,6},{6,5},{7,4},{8,11},{9,10},{10,... | collective-permute-start | bytes 1572872 | tf_op jit(solution)/shard_map/ppermute | solution.py:142
Sparse Core Ops, SparseCore 0:
  56.8 86.0 all-gather.2
